TPU v7x, 512 devices: a whole 4x8x8 slice. The times are simulated.
512 devices in a mesh: blk: 64 (over z_hi, y, core), seq: 4 (over x), mp: 2 (over z_lo).
Axes of the slice: x: 4, y: 8, z: 8 (z_hi: 4, z_lo: 2; z = z_hi * 2 + z_lo), core: 2. Of those that a mesh axis runs over, the one named last changes fastest.
Arguments:
- hidden: bfloat16 [8, 512, 1536], P(('mp', 'seq'), 'blk'), parts along dimension 0, may hold values from -6 to 6
- labels: int32 [4, 512], P('seq'), may hold values from 0 to 50303
- lengths: int32 [4, 8], P('seq'), may hold values from 1 to 256, 512 in all within a row
- owners: int32 [32], replicated, may hold values from 0 to 31, each once
- w_inner: bfloat16 [3072, 2, 3072], P('mp', None, 'blk'), parts along dimension 0, may hold values from -0.15625 to 0.15625
- w_bcdt: bfloat16 [3072, 304], P('mp'), parts along dimension 0, may hold values from -0.15625 to 0.15625
- conv_inner: float32 [8, 3072], P('mp', 'blk'), parts along dimension 0, may hold values from -3 to 3
- conv_bc: float32 [8, 256], P('mp'), parts along dimension 0, may hold values from -3 to 3
- dt_bias: float32 [96], P('mp'), parts along dimension 0, may hold values from -3 to 0.5
- decay_rate: float32 [96], P('mp'), parts along dimension 0, may hold values from 0.01 to 1
- d_skip: float32 [96], P('mp'), parts along dimension 0, may hold values from 0.5 to 2
- norm_gain: float32 [6144], P(('mp', 'blk')), parts along dimension 0, may hold values from 0.5 to 1.5
- w_out: bfloat16 [6144, 1536], P(('mp', 'blk')), parts along dimension 0, may hold values from -0.109375 to 0.109375
- final_gain: float32 [3072], P('mp'), parts along dimension 0, may hold values from 0.5 to 1.5
- w_head: bfloat16 [3072, 50304], P('mp', 'blk'), parts along dimension 0, may hold values from -0.33170174 to 0.33170174
Outputs:
- layer_out: bfloat16 [8, 512, 1536], P(('mp', 'seq'), 'blk'), parts along dimension 0
- token_logprob: float32 [8, 512], P(('mp', 'seq'), 'blk'), parts along dimension 0
- seq_logprob: float32 [64], P(('mp', 'seq')), parts along dimension 0
There are 2 independent parts, one for each index of `mp`. A program takes and returns all parts, laid end to end along the dimension named above; an argument that names none is the same for every part. Nothing has to cross between parts.
Inputs may be any that keep to these rules, and one draw needn't show every extreme that they name: The 8 lengths of a group sum to 512 and the longest is exactly 256. `owners`: every output slot is named once.
All inputs are finite; a program needn't handle non-finite values.
Results may differ from a plain program's by a relative error of at most 0.0055.
Values may be sent and summed in bfloat16 or wider, within the bound.
No kernel may reach another device: no remote copies, remote signals or barrier semaphores. Data moves between devices by JAX's collectives and lax.ppermute only.
A program may use at most 64 MiB of HBM per device.

v0:
```python
import jax
import jax.numpy as jnp
from jax import lax
from jax.sharding import PartitionSpec as P

D = 1536
HEADDIM = 64
NSTATE = 128
SCAN_BLOCK = 256
CONV = 4
EPSILON = 1e-05
HIGH = lax.Precision.HIGHEST


def segments_of(lengths, count):
    starts = jnp.cumsum(lengths, axis=-1) - lengths
    places = jnp.arange(count, dtype=jnp.int32)
    segment = jnp.sum((places[:, None] >= starts[None, :]).astype(jnp.int32), axis=-1) - 1
    first = jnp.take(starts, segment)
    return (segment, places - first)


def causal_conv(values, weights, position):
    total = values * weights[0]
    for shift_by in range(1, CONV):
        moved = jnp.concatenate(
            [jnp.zeros_like(values[:shift_by, :]), values[:-shift_by, :]], axis=0
        )
        total = (
            total + moved * weights[shift_by] * (position >= shift_by).astype(jnp.float32)[:, None]
        )
    return total


def final_norm(values, gain):
    widened = values.astype(jnp.float32)
    scale = lax.rsqrt(jnp.mean(widened * widened, axis=-1, keepdims=True) + EPSILON)
    return (widened * scale * gain).astype(jnp.bfloat16)


def shards(
    hidden,
    labels,
    lengths,
    owners,
    w_inner,
    w_bcdt,
    conv_inner,
    conv_bc,
    dt_bias,
    decay_rate,
    d_skip,
    norm_gain,
    w_out,
    final_gain,
    w_head,
):
    rows_own = hidden[0]
    rows_count = rows_own.shape[0]
    blk_count = lax.axis_size("blk")
    blk_index = lax.axis_index("blk")
    gathered = lax.all_gather(rows_own, "blk", axis=0, tiled=True)
    tokens_all = gathered.shape[0]
    channels = w_inner.shape[2]
    inner_total = channels * blk_count
    inner_proj = jnp.dot(
        gathered, w_inner.reshape(D, 2 * channels), preferred_element_type=jnp.float32
    ).astype(jnp.bfloat16)
    state_proj = jnp.dot(gathered, w_bcdt, preferred_element_type=jnp.float32).astype(jnp.bfloat16)
    gate_half = inner_proj[:, :channels].astype(jnp.float32)
    segment, position = segments_of(lengths[0], tokens_all)
    conv_value = jax.nn.silu(
        causal_conv(inner_proj[:, channels:].astype(jnp.float32), conv_inner, position)
    )
    conv_state = jax.nn.silu(
        causal_conv(state_proj[:, : 2 * NSTATE].astype(jnp.float32), conv_bc, position)
    )
    input_map = conv_state[:, :NSTATE]
    output_map = conv_state[:, NSTATE:]
    step_size = jax.nn.softplus(state_proj[:, 2 * NSTATE :].astype(jnp.float32) + dt_bias)
    log_heads = -(step_size * decay_rate)
    first_channel = blk_index * channels
    channel_head = (first_channel + jnp.arange(channels, dtype=jnp.int32)) // HEADDIM
    head_low = first_channel // HEADDIM
    head_high = (first_channel + channels - 1) // HEADDIM
    mask_high = (channel_head == head_high).astype(jnp.float32)
    mask_low = 1.0 - mask_high
    step_pair = jnp.concatenate(
        [
            lax.dynamic_slice_in_dim(step_size, head_low, 1, 1),
            lax.dynamic_slice_in_dim(step_size, head_high, 1, 1),
        ],
        axis=1,
    )
    log_pair = jnp.concatenate(
        [
            lax.dynamic_slice_in_dim(log_heads, head_low, 1, 1),
            lax.dynamic_slice_in_dim(log_heads, head_high, 1, 1),
        ],
        axis=1,
    )
    step_channel = step_pair[:, 0:1] * mask_low + step_pair[:, 1:2] * mask_high
    driven = conv_value * step_channel
    slot_masks = (mask_low, mask_high)
    blocks = tokens_all // SCAN_BLOCK
    order = jnp.arange(SCAN_BLOCK, dtype=jnp.int32)
    causal = order[:, None] >= order[None, :]

    def block_step(carry, inputs):
        carried, previous = carry
        drive_block, in_block, out_block, log_block, seg_block = inputs
        cumulative = jnp.cumsum(log_block, axis=0)
        gram = jnp.dot(out_block, in_block.T, precision=HIGH)
        same = (seg_block[:, None] == seg_block[None, :]) & causal
        result = jnp.zeros((SCAN_BLOCK, channels), jnp.float32)
        for slot_index in range(2):
            column = cumulative[:, slot_index]
            spread = jnp.minimum(column[:, None] - column[None, :], 0.0)
            weights = jnp.where(same, jnp.exp(spread), 0.0)
            result = result + jnp.dot(
                gram * weights, drive_block * slot_masks[slot_index], precision=HIGH
            )
        carried_in = carried * (seg_block[0] == previous).astype(jnp.float32)
        rising = jnp.exp(cumulative[:, 0:1]) * mask_low + jnp.exp(cumulative[:, 1:2]) * mask_high
        leading = (seg_block == seg_block[0]).astype(jnp.float32)[:, None]
        result = result + leading * rising * jnp.dot(out_block, carried_in.T, precision=HIGH)
        trailing = (seg_block == seg_block[-1]).astype(jnp.float32)[:, None]
        tail_low = jnp.exp(cumulative[-1:, 0:1] - cumulative[:, 0:1])
        tail_high = jnp.exp(cumulative[-1:, 1:2] - cumulative[:, 1:2])
        tail = tail_low * mask_low + tail_high * mask_high
        whole_block = (seg_block[-1] == seg_block[0]).astype(jnp.float32)
        carried_new = whole_block * rising[-1][:, None] * carried_in + jnp.dot(
            (drive_block * tail * trailing).T, in_block, precision=HIGH
        )
        return ((carried_new, seg_block[-1]), result)

    initial = (jnp.zeros((channels, NSTATE), jnp.float32), jnp.int32(-1))
    scan_inputs = (
        driven.reshape(blocks, SCAN_BLOCK, channels),
        input_map.reshape(blocks, SCAN_BLOCK, NSTATE),
        output_map.reshape(blocks, SCAN_BLOCK, NSTATE),
        log_pair.reshape(blocks, SCAN_BLOCK, 2),
        segment.reshape(blocks, SCAN_BLOCK),
    )
    final_carry, scanned = lax.scan(block_step, initial, scan_inputs)
    mixed = scanned.reshape(tokens_all, channels) + jnp.take(d_skip, channel_head) * conv_value
    gated = mixed * jax.nn.silu(gate_half)
    squares = lax.psum(jnp.sum(gated * gated, axis=1), "blk")
    inverse = lax.rsqrt(squares / inner_total + EPSILON)
    gated_norm = (gated * inverse[:, None] * norm_gain).astype(jnp.bfloat16)
    delta_own = lax.psum_scatter(
        jnp.dot(gated_norm, w_out, preferred_element_type=jnp.float32),
        "blk",
        scatter_dimension=0,
        tiled=True,
    )
    layer_own = (rows_own.astype(jnp.float32) + delta_own).astype(jnp.bfloat16)
    logits = jnp.dot(
        lax.all_gather(final_norm(layer_own, final_gain), "blk", axis=0, tiled=True),
        w_head,
        preferred_element_type=jnp.float32,
    )
    vocab_local = w_head.shape[1]
    local_label = labels[0] - blk_index * vocab_local
    hit = jnp.arange(vocab_local, dtype=jnp.int32)[None, :] == local_label[:, None]
    target_local = jnp.sum(jnp.where(hit, logits, 0.0), axis=1)
    top_local = jnp.max(logits, axis=1)
    top_all = lax.pmax(top_local, "blk")
    expsum_local = jnp.sum(jnp.exp(logits - top_all[:, None]), axis=1)
    expsum_all, target_all = lax.psum((expsum_local, target_local), "blk")
    logprob = target_all - (top_all + jnp.log(expsum_all))
    token_own = lax.dynamic_slice_in_dim(logprob, blk_index * rows_count, rows_count, 0)
    seqs_count = lengths.shape[1]
    onehot = (segment[:, None] == jnp.arange(seqs_count, dtype=jnp.int32)[None, :]).astype(
        jnp.float32
    )
    sums = jnp.dot(logprob, onehot, precision=HIGH)
    seq_index = lax.axis_index("seq")
    mine = lax.dynamic_slice_in_dim(owners, seq_index * seqs_count, seqs_count, 0)
    placement = (mine[:, None] == jnp.arange(owners.shape[0], dtype=jnp.int32)[None, :]).astype(
        jnp.float32
    )
    spread_sums = jnp.dot(sums, placement, precision=HIGH)
    seq_own = lax.psum_scatter(spread_sums, "seq", scatter_dimension=0, tiled=True)
    return (layer_own[None], token_own[None], seq_own)


def solution(mesh):
    in_specs = (
        P(("mp", "seq"), "blk", None),
        P("seq", None),
        P("seq", None),
        P(),
        P("mp", None, "blk"),
        P("mp", None),
        P("mp", "blk"),
        P("mp", None),
        P("mp"),
        P("mp"),
        P("mp"),
        P(("mp", "blk")),
        P(("mp", "blk"), None),
        P("mp"),
        P("mp", "blk"),
    )
    out_specs = (P(("mp", "seq"), "blk", None), P(("mp", "seq"), "blk"), P(("mp", "seq")))
    return jax.shard_map(shards, mesh=mesh, in_specs=in_specs, out_specs=out_specs, check_vma=False)
```

profile of v0, /device:TPU:1, one launch (start us, length us, event | category | flops | bytes accessed | tf_op | source)
XLA Modules:
  0.0 819.6 jit_solution(5413940078656478816)
XLA Ops:
  8.0 0.8 reduce-window.10
  10.2 1.4 gather_fusion
  13.6 1.4 slice_bitcast_fusion.3
  15.0 4.4 compare_select_fusion.5
  20.1 0.8 fusion.99
  21.0 80.3 %all-gather.6.cloned.1.call-done = bf16[1,512,1536]{2,1,0:T(8,128)(2,1)} async-done(((bf16[1,8,1536]{2,1,0:T(8,128)(2,1)}), bf16[1,512,1536]{2,1,0:T(8,128)(2,1)}) %all-gather.6.cloned.1.call-update) | async-done | bytes 1572880 | tf_op jit(solution)/shard_map/all_gather | solution.py:62
  101.3 2.3 fusion.71
  104.8 2.0 fusion.74
  108.1 29.1 %while.17 = (s32[]{:T(128)}, f32[48,128]{1,0:T(8,128)S(1)}, s32[]{:T(128)}, f32[2,256,48]{1,0,2:T(2,128)}, s32[2,256]{1,0:T(2,128)}, /*index=5*/f32[2,256,2]{1,2...) while((s32[]{:T(128)}, f32[48,128]{1,0:T(8,128)S(1)}, ...), condition=%wide.region_5.6_spmd.clone.clone.clone, body=%wide.region_2.5_spmd.clone.clone.clone.sunk | while | flops 215140816 | bytes 2177448 | solution.py:145
  108.1 0.7 dynamic-slice_bitcast_fusion.3
  110.4 1.3 fusion.130
  113.8 1.3 constant_dynamic-slice_fusion.12
  115.1 1.9 compare_convert_fusion.10
  118.0 2.2 dynamic_update_slice.8
  122.6 0.7 dynamic-slice_bitcast_fusion.3
  125.0 1.3 fusion.130
  128.4 1.3 constant_dynamic-slice_fusion.12
  129.6 1.9 compare_convert_fusion.10
  132.5 2.2 dynamic_update_slice.8
  137.2 0.9 copy.54
  138.1 0.7 multiply_reduce_fusion
  138.8 138.1 %psum.21 = f32[512]{0:T(512)S(1)} all-reduce(f32[512]{0:T(512)S(1)} %get-tuple-element.251), channel_id=1, replica_groups=mesh['blk'=64,'seq'=4,'mp'=2] {'blk'}, use_global_device_ids=true, to_apply=%region_7.8 | all-reduce | flops 512 | bytes 4096 | tf_op jit(solution)/shard_map/psum | solution.py:148
  276.9 3.0 fusion.85
  279.9 148.0 %reduce-scatter.2.cloned.1.call-done = f32[8,1536]{1,0:T(8,128)} async-done(((f32[512,1536]{1,0:T(8,128)}), f32[8,1536]{1,0:T(8,128)}) %reduce-scatter.2.cloned.1.call-update) | async-done | bytes 49168 | tf_op jit(solution)/shard_map/reduce_scatter | solution.py:151
  428.0 0.9 fusion.82
  429.7 1.3 dynamic-slice
  431.7 85.4 %all-gather.4.cloned.1.call-done = bf16[512,1536]{1,0:T(8,128)(2,1)} async-done(((bf16[8,1536]{1,0:T(8,128)(2,1)}), bf16[512,1536]{1,0:T(8,128)(2,1)}) %all-gather.4.cloned.1.call-update) | async-done | bytes 1572880 | tf_op jit(solution)/shard_map/all_gather | solution.py:159
  517.1 4.0 fusion.101
  521.1 138.1 %pmax.7 = f32[512]{0:T(512)S(1)} all-reduce(f32[512]{0:T(512)S(1)} %get-tuple-element.299), channel_id=1, replica_groups=mesh['blk'=64,'seq'=4,'mp'=2] {'blk'}, use_global_device_ids=true, to_apply=%region_13.14 | all-reduce | flops 512 | bytes 4096 | tf_op jit(solution)/shard_map/pmax | solution.py:168
  659.2 1.9 exponential_reduce_fusion
  661.1 142.0 %all-reduce.7 = (f32[512]{0:T(512)S(1)}, f32[512]{0:T(512)S(1)}) all-reduce(f32[512]{0:T(512)S(1)} %get-tuple-element.222, f32[512]{0:T(512)S(1)} %get-tuple-element.221), channel_id=1, replica_groups=mesh['blk'=64,'seq'=4,'mp'=2] {'blk'}, use_global_device_ids=true, to_apply=%region_11.12 | all-reduce | flops 1024 | bytes 8192 | tf_op jit(solution)/shard_map/psum | solution.py:170
  803.6 8.4 %all-reduce.6 = f32[32]{0:T(128)S(1)} all-reduce(f32[32]{0:T(128)S(1)} %convolution_bitcast_fusion.1), channel_id=4, replica_groups=mesh['blk'=64,'seq'=4,'mp'=2] {'seq'}, use_global_device_ids=true, to_apply=%region_16.17.clone | all-reduce | flops 32 | bytes 256
  (127 shorter events, 18.5 us)
Async XLA Ops:
  7.2 509.9 %copy-start = (bf16[1536,786]{0,1:T(8,128)(2,1)S(1)}, bf16[1536,786]{0,1:T(8,128)(2,1)}, u32[]{:S(2)}) copy-start(bf16[1536,786]{0,1:T(8,128)(2,1)} %param.31) | copy-start | bytes 7243780
  7.2 94.1 %all-gather.6.cloned.1.call-start = ((), (), s32[]{:S(2)}) async-start(), calls=%async_computation.3 | async-start | bytes 1597440 | tf_op jit(solution)/shard_map/all_gather | solution.py:62
  7.9 420.1 %reduce-scatter.2.cloned.1.call-start = ((), (), s32[]{:S(2)}) async-start(), calls=%async_computation.1 | async-start | bytes 3194880 | tf_op jit(solution)/shard_map/reduce_scatter | solution.py:151
  9.6 94.1 %copy-start.5 = (s32[512]{0:T(512)}, s32[512]{0:T(512)S(1)}, u32[]{:S(2)}) copy-start(s32[512]{0:T(512)S(1)} %get-tuple-element.290) | copy-start | bytes 6148
  20.1 83.6 %copy-start.11 = (f32[512]{0:T(512)}, f32[512]{0:T(512)S(1)}, u32[]{:S(2)}) copy-start(f32[512]{0:T(512)S(1)} %get-tuple-element.257) | copy-start | bytes 6148
  20.1 83.6 %copy-start.7 = (f32[512]{0:T(512)}, f32[512]{0:T(512)S(1)}, u32[]{:S(2)}) copy-start(f32[512]{0:T(512)S(1)} %get-tuple-element.287) | copy-start | bytes 6148
  20.1 83.6 %copy-start.9 = (f32[512]{0:T(512)}, f32[512]{0:T(512)S(1)}, u32[]{:S(2)}) copy-start(f32[512]{0:T(512)S(1)} %get-tuple-element.288) | copy-start | bytes 6148
  104.7 2.2 copy-start.21
  104.7 2.2 copy-start.22
  104.7 2.3 copy-start.8
  104.7 2.3 copy-start.10
  104.8 2.3 copy-start.12
  104.8 2.3 copy-start.15
  104.8 2.3 copy-start.16
  104.8 2.3 copy-start.17
  104.8 2.3 copy-start.18
  104.8 2.3 copy-start.19
  104.8 2.3 copy-start.20
  108.1 168.8 %copy-start.1 = (bf16[48,1536]{1,0:T(8,128)(2,1)S(1)}, bf16[48,1536]{1,0:T(8,128)(2,1)}, u32[]{:S(2)}) copy-start(bf16[48,1536]{1,0:T(8,128)(2,1)} %param.29) | copy-start | bytes 442372
  112.8 1.0 copy-start.2
  127.3 1.0 copy-start.2
  279.9 148.1 %copy-start.4 = (bf16[1,8,1536]{2,1,0:T(8,128)(2,1)S(1)}, bf16[1,8,1536]{2,1,0:T(8,128)(2,1)}, u32[]{:S(2)}) copy-start(bf16[1,8,1536]{2,1,0:T(8,128)(2,1)} %param.17) | copy-start | bytes 73732
  279.9 149.1 %copy-start.13 = (f32[1536]{0:T(1024)S(1)}, f32[1536]{0:T(1024)}, u32[]{:S(2)}) copy-start(f32[1536]{0:T(1024)} %param.30) | copy-start | bytes 18436
  279.9 149.8 %copy-start.23 = (s32[32]{0:T(128)S(1)}, s32[32]{0:T(128)}, u32[]{:S(2)}) copy-start(s32[32]{0:T(128)} %param.20) | copy-start | bytes 388
  279.9 151.8 %copy-start.14 = (s32[1,512]{1,0:T(1,128)S(1)}, s32[1,512]{1,0:T(1,128)}, u32[]{:S(2)}) copy-start(s32[1,512]{1,0:T(1,128)} %param.18) | copy-start | bytes 6148
  279.9 237.2 %all-gather.4.cloned.1.call-start = ((), (), s32[]{:S(2)}) async-start(), calls=%async_computation.2 | async-start | bytes 1597440 | tf_op jit(solution)/shard_map/all_gather | solution.py:159
  428.9 92.2 %copy-start.3 = (bf16[8,1536]{1,0:T(8,128)(2,1)}, bf16[8,1536]{1,0:T(8,128)(2,1)S(1)}, u32[]{:S(2)}) copy-start(bf16[8,1536]{1,0:T(8,128)(2,1)S(1)} %get-tuple-element.250) | copy-start | bytes 73732
  521.1 282.0 %copy-start.6 = (s32[512]{0:T(512)S(1)}, s32[512]{0:T(512)}, u32[]{:S(2)}) copy-start(s32[512]{0:T(512)} %copy-done.5) | copy-start | bytes 6148
Sparse Core Ops, SparseCore 0:
  11.3 89.9 all-gather.5
  280.0 147.9 reduce-scatter.1
  431.3 85.7 all-gather.3
where the time goes:
time: 821 us; the launch traced here: 820 us
  blocking collectives  427 us (52%)
  waiting for transfers between devices  314 us (38%)
  other arithmetic  22.4 us (3%)
  local copies, waits for them, and re-layouts  20.4 us (2%)
  matrix products  15.5 us (2%)
  between operations  14.9 us (2%)
    reduce_scatter x1, waiting for transfers between devices, shards(): lax.psum_scatter(jnp.dot(gated_norm, w_out, preferred_element_type=jnp.fl...  148 us
    psum x1, blocking collectives, shards(): expsum_all, target_all = lax.psum((expsum_local, target_local), 'blk')  142 us
    psum x1, blocking collectives, shards(): squares = lax.psum(jnp.sum(gated * gated, axis=1), 'blk')  138 us
    pmax x1, blocking collectives, shards(): top_all = lax.pmax(top_local, 'blk')  138 us
    all_gather x1, waiting for transfers between devices, shards(): lax.all_gather(final_norm(layer_own, final_gain), 'blk', axis=0, tiled=True)  85.4 us
    all_gather x1, waiting for transfers between devices, shards(): gathered = lax.all_gather(rows_own, 'blk', axis=0, tiled=True)  80.3 us
  transfers between devices with their start and end apart: 3, of which 3 were waited for; matrix products, arithmetic and copies ran while one was open for 2% of the time, Pallas kernels for 0%

commit v1 on v0

--- a/solution.py
+++ b/solution.py
@@ -145,7 +145,7 @@
     final_carry, scanned = lax.scan(block_step, initial, scan_inputs)
     mixed = scanned.reshape(tokens_all, channels) + jnp.take(d_skip, channel_head) * conv_value
     gated = mixed * jax.nn.silu(gate_half)
-    squares = lax.psum(jnp.sum(gated * gated, axis=1), "blk")
+    squares = jnp.sum(lax.all_gather(jnp.sum(gated * gated, axis=1), "blk"), axis=0)
     inverse = lax.rsqrt(squares / inner_total + EPSILON)
     gated_norm = (gated * inverse[:, None] * norm_gain).astype(jnp.bfloat16)
     delta_own = lax.psum_scatter(

time: 821 us -> 759 us (0.924)
  blocking collectives: 427 us -> 369 us
    psum x1 -> x0, blocking collectives: 138 us -> none  [shards(): squares = lax.psum(jnp.sum(gated * gated, axis=1), 'blk')]
    all_gather x0 -> x1, blocking collectives: none -> 80.3 us  [shards(): lax.all_gather(jnp.sum(gated * gated, axis=1), 'blk')]
where the time goes in v1:
time: 759 us; the launch traced here: 758 us
  blocking collectives  369 us (49%)
  waiting for transfers between devices  310 us (41%)
  other arithmetic  22.6 us (3%)
  local copies, waits for them, and re-layouts  20.4 us (3%)
  matrix products  15.5 us (2%)
  between operations  14.9 us (2%)
    reduce_scatter x1, waiting for transfers between devices, shards(): lax.psum_scatter(jnp.dot(gated_norm, w_out, preferred_element_type=jnp.fl...  144 us
    psum x1, blocking collectives, shards(): expsum_all, target_all = lax.psum((expsum_local, target_local), 'blk')  142 us
    pmax x1, blocking collectives, shards(): top_all = lax.pmax(top_local, 'blk')  138 us
    all_gather x1, waiting for transfers between devices, shards(): lax.all_gather(final_norm(layer_own, final_gain), 'blk', axis=0, tiled=True)  85.4 us
    all_gather x1, blocking collectives, shards(): lax.all_gather(jnp.sum(gated * gated, axis=1), 'blk')  80.3 us
    all_gather x1, waiting for transfers between devices, shards(): gathered = lax.all_gather(rows_own, 'blk', axis=0, tiled=True)  80.3 us
  transfers between devices with their start and end apart: 3, of which 3 were waited for; matrix products, arithmetic and copies ran while one was open for 2% of the time, Pallas kernels for 0%

profile of v1, /device:TPU:1, one launch (start us, length us, event | category | flops | bytes accessed | tf_op | source)
XLA Modules:
  0.0 757.7 jit_solution(9265564906531698834)
XLA Ops:
  8.0 0.8 reduce-window.10
  10.2 1.4 gather_fusion
  13.6 1.4 slice_bitcast_fusion.3
  15.0 4.4 compare_select_fusion.5
  20.1 0.8 fusion.99
  21.0 80.3 %all-gather.8.cloned.1.call-done = bf16[1,512,1536]{2,1,0:T(8,128)(2,1)} async-done(((bf16[1,8,1536]{2,1,0:T(8,128)(2,1)}), bf16[1,512,1536]{2,1,0:T(8,128)(2,1)}) %all-gather.8.cloned.1.call-update) | async-done | bytes 1572880 | tf_op jit(solution)/shard_map/all_gather | solution.py:62
  101.3 2.3 fusion.71
  104.8 2.0 fusion.74
  108.1 29.1 %while.17 = (s32[]{:T(128)}, f32[48,128]{1,0:T(8,128)S(1)}, s32[]{:T(128)}, f32[2,256,48]{1,0,2:T(2,128)}, s32[2,256]{1,0:T(2,128)}, /*index=5*/f32[2,256,2]{1,2...) while((s32[]{:T(128)}, f32[48,128]{1,0:T(8,128)S(1)}, ...), condition=%wide.region_5.6_spmd.clone.clone.clone, body=%wide.region_2.5_spmd.clone.clone.clone.sunk | while | flops 215140816 | bytes 2177448 | solution.py:145
  108.1 0.7 dynamic-slice_bitcast_fusion.3
  110.5 1.3 fusion.130
  113.8 1.3 constant_dynamic-slice_fusion.12
  115.1 1.9 compare_convert_fusion.10
  118.0 2.2 dynamic_update_slice.8
  122.7 0.7 dynamic-slice_bitcast_fusion.3
  125.0 1.3 fusion.130
  128.4 1.3 constant_dynamic-slice_fusion.12
  129.6 1.9 compare_convert_fusion.10
  132.5 2.2 dynamic_update_slice.8
  137.2 0.9 copy.55
  138.1 0.7 multiply_reduce_fusion
  138.8 80.3 %all-gather.2 = f32[64,1,512]{2,1,0:T(1,128)S(1)} all-gather(f32[1,1,512]{2,1,0:T(1,128)S(1)} %bitcast.208), channel_id=3, replica_groups=mesh['blk'=64,'seq'=4,'mp'=2] {'blk'}, dimensions={0}, use_global_device_ids=true | all-gather | bytes 133120 | tf_op jit(solution)/shard_map/all_gather | solution.py:148
  219.3 3.0 fusion.85
  222.3 143.8 %reduce-scatter.2.cloned.1.call-done = f32[8,1536]{1,0:T(8,128)} async-done(((f32[512,1536]{1,0:T(8,128)}), f32[8,1536]{1,0:T(8,128)}) %reduce-scatter.2.cloned.1.call-update) | async-done | bytes 49168 | tf_op jit(solution)/shard_map/reduce_scatter | solution.py:151
  366.1 0.9 fusion.82
  367.8 1.3 dynamic-slice
  369.8 85.4 %all-gather.6.cloned.1.call-done = bf16[512,1536]{1,0:T(8,128)(2,1)} async-done(((bf16[8,1536]{1,0:T(8,128)(2,1)}), bf16[512,1536]{1,0:T(8,128)(2,1)}) %all-gather.6.cloned.1.call-update) | async-done | bytes 1572880 | tf_op jit(solution)/shard_map/all_gather | solution.py:159
  455.2 4.0 fusion.101
  459.2 138.1 %pmax.7 = f32[512]{0:T(512)S(1)} all-reduce(f32[512]{0:T(512)S(1)} %get-tuple-element.299), channel_id=1, replica_groups=mesh['blk'=64,'seq'=4,'mp'=2] {'blk'}, use_global_device_ids=true, to_apply=%region_13.14 | all-reduce | flops 512 | bytes 4096 | tf_op jit(solution)/shard_map/pmax | solution.py:168
  597.3 1.9 exponential_reduce_fusion
  599.1 142.0 %all-reduce.7 = (f32[512]{0:T(512)S(1)}, f32[512]{0:T(512)S(1)}) all-reduce(f32[512]{0:T(512)S(1)} %get-tuple-element.222, f32[512]{0:T(512)S(1)} %get-tuple-element.221), channel_id=1, replica_groups=mesh['blk'=64,'seq'=4,'mp'=2] {'blk'}, use_global_device_ids=true, to_apply=%region_11.12 | all-reduce | flops 1024 | bytes 8192 | tf_op jit(solution)/shard_map/psum | solution.py:170
  741.6 8.4 %all-reduce.6 = f32[32]{0:T(128)S(1)} all-reduce(f32[32]{0:T(128)S(1)} %convolution_bitcast_fusion.1), channel_id=5, replica_groups=mesh['blk'=64,'seq'=4,'mp'=2] {'seq'}, use_global_device_ids=true, to_apply=%region_16.17.clone | all-reduce | flops 32 | bytes 256
  (128 shorter events, 18.6 us)
Async XLA Ops:
  7.2 448.0 %copy-start = (bf16[1536,786]{0,1:T(8,128)(2,1)S(1)}, bf16[1536,786]{0,1:T(8,128)(2,1)}, u32[]{:S(2)}) copy-start(bf16[1536,786]{0,1:T(8,128)(2,1)} %param.31) | copy-start | bytes 7243780
  7.2 94.1 %all-gather.8.cloned.1.call-start = ((), (), s32[]{:S(2)}) async-start(), calls=%async_computation.3 | async-start | bytes 1597440 | tf_op jit(solution)/shard_map/all_gather | solution.py:62
  7.9 358.2 %reduce-scatter.2.cloned.1.call-start = ((), (), s32[]{:S(2)}) async-start(), calls=%async_computation.1 | async-start | bytes 3194880 | tf_op jit(solution)/shard_map/reduce_scatter | solution.py:151
  9.6 94.1 %copy-start.5 = (s32[512]{0:T(512)}, s32[512]{0:T(512)S(1)}, u32[]{:S(2)}) copy-start(s32[512]{0:T(512)S(1)} %get-tuple-element.290) | copy-start | bytes 6148
  20.1 83.6 %copy-start.11 = (f32[512]{0:T(512)}, f32[512]{0:T(512)S(1)}, u32[]{:S(2)}) copy-start(f32[512]{0:T(512)S(1)} %get-tuple-element.257) | copy-start | bytes 6148
  20.1 83.6 %copy-start.7 = (f32[512]{0:T(512)}, f32[512]{0:T(512)S(1)}, u32[]{:S(2)}) copy-start(f32[512]{0:T(512)S(1)} %get-tuple-element.287) | copy-start | bytes 6148
  20.1 83.6 %copy-start.9 = (f32[512]{0:T(512)}, f32[512]{0:T(512)S(1)}, u32[]{:S(2)}) copy-start(f32[512]{0:T(512)S(1)} %get-tuple-element.288) | copy-start | bytes 6148
  104.7 2.2 copy-start.21
  104.7 2.2 copy-start.22
  104.8 2.3 copy-start.8
  104.8 2.3 copy-start.10
  104.8 2.3 copy-start.12
  104.8 2.3 copy-start.15
  104.8 2.3 copy-start.16
  104.8 2.3 copy-start.17
  104.8 2.3 copy-start.18
  104.8 2.3 copy-start.19
  104.8 2.3 copy-start.20
  108.1 111.2 %copy-start.1 = (bf16[48,1536]{1,0:T(8,128)(2,1)S(1)}, bf16[48,1536]{1,0:T(8,128)(2,1)}, u32[]{:S(2)}) copy-start(bf16[48,1536]{1,0:T(8,128)(2,1)} %param.29) | copy-start | bytes 442372
  112.8 1.0 copy-start.2
  127.3 1.0 copy-start.2
  222.2 143.9 %copy-start.4 = (bf16[1,8,1536]{2,1,0:T(8,128)(2,1)S(1)}, bf16[1,8,1536]{2,1,0:T(8,128)(2,1)}, u32[]{:S(2)}) copy-start(bf16[1,8,1536]{2,1,0:T(8,128)(2,1)} %param.17) | copy-start | bytes 73732
  222.2 144.8 %copy-start.13 = (f32[1536]{0:T(1024)S(1)}, f32[1536]{0:T(1024)}, u32[]{:S(2)}) copy-start(f32[1536]{0:T(1024)} %param.30) | copy-start | bytes 18436
  222.2 145.5 %copy-start.23 = (s32[32]{0:T(128)S(1)}, s32[32]{0:T(128)}, u32[]{:S(2)}) copy-start(s32[32]{0:T(128)} %param.20) | copy-start | bytes 388
  222.2 147.5 %copy-start.14 = (s32[1,512]{1,0:T(1,128)S(1)}, s32[1,512]{1,0:T(1,128)}, u32[]{:S(2)}) copy-start(s32[1,512]{1,0:T(1,128)} %param.18) | copy-start | bytes 6148
  222.3 232.9 %all-gather.6.cloned.1.call-start = ((), (), s32[]{:S(2)}) async-start(), calls=%async_computation.2 | async-start | bytes 1597440 | tf_op jit(solution)/shard_map/all_gather | solution.py:159
  367.0 92.2 %copy-start.3 = (bf16[8,1536]{1,0:T(8,128)(2,1)}, bf16[8,1536]{1,0:T(8,128)(2,1)S(1)}, u32[]{:S(2)}) copy-start(bf16[8,1536]{1,0:T(8,128)(2,1)S(1)} %get-tuple-element.250) | copy-start | bytes 73732
  459.2 282.0 %copy-start.6 = (s32[512]{0:T(512)S(1)}, s32[512]{0:T(512)}, u32[]{:S(2)}) copy-start(s32[512]{0:T(512)} %copy-done.5) | copy-start | bytes 6148
Sparse Core Ops, SparseCore 0:
  11.3 89.9 all-gather.7
  222.4 143.6 reduce-scatter.1
  369.4 85.7 all-gather.5
